TPU v7x, 512 devices: a whole 4x8x8 slice. The times are simulated.
512 devices in a mesh: section: 8 (over y), expert: 32 (over z, x_hi, core), dp: 2 (over x_lo).
Axes of the slice: x: 4 (x_hi: 2, x_lo: 2; x = x_hi * 2 + x_lo), y: 8, z: 8, core: 2. Of those that a mesh axis runs over, the one named last changes fastest.
Arguments:
- blocks: bfloat16 [8, 512, 7168], P('section', ('expert', 'dp')), may hold values from -6 to 6
- gains: float32 [8, 7168], P('section'), may hold values from 0.1 to 1.9
- w_gate: bfloat16 [8, 7168, 4096], P('section', 'dp', 'expert'), may hold values from -0.0625 to 0.0625
- w_up: bfloat16 [8, 7168, 4096], P('section', 'dp', 'expert'), may hold values from -0.0625 to 0.0625
- w_down: bfloat16 [8, 7168, 4096], P('section', 'dp', 'expert'), may hold values from -0.1875 to 0.1875
- expert_ids: int32 [8, 2, 512, 2], P('section', None, ('expert', 'dp')), may hold values from 0 to 3, all different within a row; in each aligned block of 8 rows (0 to 7, 8 to 15, ..., all dimensions but the last counted through in order) at most 5 rows name the same one
- combine: float32 [8, 2, 512, 2], P('section', None, ('expert', 'dp')), may hold values from 0.2 to 1
Outputs:
- finished: bfloat16 [8, 512, 7168], P('section', ('expert', 'dp'))
Inputs may be any that keep to these rules, and one draw needn't show every extreme that they name: `expert_ids`: each token names 2 different experts; within the 8 tokens of one device (aligned blocks), no expert is named more than 5 times, a bound that some block reaches.
All inputs are finite; a program needn't handle non-finite values.
Results may differ from a plain program's by a relative error of at most 0.0073.
Values may be sent and summed in bfloat16 or wider, within the bound.
No kernel may reach another device: no remote copies, remote signals or barrier semaphores. Data moves between devices by JAX's collectives and lax.ppermute only.
A program may use at most 64 MiB of HBM per device.

v0:
```python
from functools import partial
import jax
import jax.numpy as jnp
import numpy as np
from jax import lax
from jax.sharding import Mesh
from jax.sharding import PartitionSpec as P

ALL = ("eg", "q", "dp")


def passed_along(array, axis, by):
    length = lax.axis_size(axis)
    return lax.ppermute(array, axis, [(i, (i + by) % length) for i in range(length)])


def route(stream, gain_row, routes, experts, capacity):
    tok_rows, model_width = stream.shape
    fan_out = routes.shape[1]
    widened = stream.astype(jnp.float32)
    inv_rms = lax.rsqrt(jnp.mean(widened * widened, axis=1, keepdims=True) + 1e-06)
    normed = (widened * inv_rms * gain_row[None, :]).astype(jnp.bfloat16)
    flat_ids = routes.reshape(-1)
    count_all = flat_ids.shape[0]
    chosen = (flat_ids[:, None] == jnp.arange(experts, dtype=jnp.int32)[None, :]).astype(
        jnp.float32
    )
    triangle = (jnp.arange(count_all)[:, None] >= jnp.arange(count_all)[None, :]).astype(
        jnp.float32
    )
    running = jnp.dot(triangle, chosen, preferred_element_type=jnp.float32)
    slot_of = jnp.sum(chosen * (running - 1.0), axis=1).astype(jnp.int32)
    target = flat_ids * capacity + slot_of
    placing = jnp.arange(experts * capacity, dtype=jnp.int32)[:, None] == target[None, :]
    placing = (
        placing.reshape(experts * capacity, tok_rows, fan_out).any(axis=2).astype(jnp.bfloat16)
    )
    outgoing = jnp.dot(placing, normed, preferred_element_type=jnp.float32).astype(jnp.bfloat16)
    return (widened, outgoing.reshape(experts, capacity, model_width), target)


def moe_layer(stream, gain_row, gate_w, up_w, down_mine, routes, mixing):
    experts = lax.axis_size("eg")
    blocks = lax.axis_size("q")
    halves = lax.axis_size("dp")
    tok_rows, model_width = stream.shape
    fan_out = routes.shape[1]
    capacity = min(tok_rows, max(2, 5 * tok_rows * fan_out // (4 * experts)))
    half = model_width // halves
    widened, outgoing, target = route(stream, gain_row, routes, experts, capacity)
    lanes = 128
    tiles = half // lanes
    send = outgoing.reshape(experts, capacity, halves, tiles, lanes).transpose(0, 2, 1, 3, 4)
    send = send.reshape(experts * halves, 2, capacity * half // 2)
    arrived = lax.all_to_all(send, ("eg", "dp"), split_axis=0, concat_axis=0, tiled=True)
    arrived = arrived.reshape(experts * halves, capacity, half).transpose(1, 0, 2)
    arrived = lax.all_gather(arrived, "q", axis=1, tiled=True)
    sources = blocks * experts * halves
    rows = arrived.reshape(capacity * sources, half)
    units = gate_w.shape[1]
    both_w = jnp.concatenate([gate_w, up_w], axis=1)
    gate_up = jnp.dot(rows, both_w, preferred_element_type=jnp.float32)
    mine = gate_up.reshape(rows.shape[0], 2, units).transpose(1, 0, 2)
    both = mine + passed_along(mine.astype(jnp.bfloat16), "dp", 1).astype(jnp.float32)
    hidden = (jax.nn.silu(both[0]) * both[1]).astype(jnp.bfloat16)
    hidden_all = lax.all_gather(hidden, "q", axis=1, tiled=True)
    out = lax.dot_general(
        hidden_all, down_mine, (((1,), (1,)), ((), ())), preferred_element_type=jnp.float32
    ).astype(jnp.bfloat16)
    piece = out.shape[1]
    out = out.reshape(capacity, blocks, experts, halves, piece).transpose(2, 1, 3, 0, 4)
    back = lax.all_to_all(
        out.reshape(sources, 2, capacity * piece // 2), ALL, split_axis=0, concat_axis=0, tiled=True
    )
    back = back.reshape(experts, blocks, halves, capacity, piece).transpose(0, 3, 2, 1, 4)
    expert_out = back.reshape(experts * capacity, model_width)
    picked = jnp.take(expert_out, target, axis=0)
    picked = picked.reshape(tok_rows, fan_out, model_width)
    mixed_sum = jnp.sum(mixing[:, :, None] * picked.astype(jnp.float32), axis=1)
    return (widened + mixed_sum).astype(jnp.bfloat16)


def on_device(blocks, gains, w_gate, w_up, w_down, expert_ids, combine):
    stream = blocks[0]
    turns = expert_ids.shape[1]
    n_blocks = lax.axis_size("q")
    down_local = w_down[0]
    half, width = down_local.shape
    piece = half // n_blocks
    down_mine = lax.all_to_all(
        down_local.reshape(n_blocks, piece, width), "q", split_axis=0, concat_axis=0, tiled=True
    )
    down_mine = down_mine.transpose(1, 0, 2).reshape(piece, n_blocks * width)
    for layer_turn in range(turns):
        if layer_turn > 0:
            stream = passed_along(stream, "section", 1)
        stream = moe_layer(
            stream,
            gains[0],
            w_gate[0],
            w_up[0],
            down_mine,
            expert_ids[0, layer_turn],
            combine[0, layer_turn],
        )
    return stream[None]


def solution(mesh):
    n_section, n_expert, n_dp = (mesh.shape[a] for a in ("section", "expert", "dp"))
    n_q = n_expert // 4
    inner = Mesh(
        np.asarray(mesh.devices).reshape(n_section, n_expert // n_q, n_q, n_dp),
        ("section", "eg", "q", "dp"),
    )
    tok = ("eg", "q", "dp")
    in_specs = (
        P("section", tok, None),
        P("section", None),
        P("section", "dp", ("eg", "q")),
        P("section", "dp", ("eg", "q")),
        P("section", "dp", ("eg", "q")),
        P("section", None, tok, None),
        P("section", None, tok, None),
    )
    out_specs = P("section", tok, None)
    return jax.shard_map(
        on_device, mesh=inner, in_specs=in_specs, out_specs=out_specs, check_vma=False
    )
```

profile of v0, /device:TPU:1, one launch (start us, length us, event | category | flops | bytes accessed | tf_op | source)
XLA Modules:
  0.0 239.1 jit_solution(17253363982797982586)
XLA Ops:
  11.7 21.9 %all_to_all.25 = bf16[8,2,8960]{2,1,0:T(2,128)(2,1)S(1)} all-to-all(bf16[8,2,8960]{2,1,0:T(2,128)(2,1)S(1)} %reshape.126), channel_id=1, replica_groups=mesh['section'=8,'eg'=4,'q'=8,'dp'=2] {'eg','dp'}, dimensions={0} | all-to-all | bytes 573440 | tf_op jit(solution)/shard_map/all_to_all | solution.py:55
  34.6 8.1 %all-to-all-start.1 = ((bf16[8,448,128]{2,1,0:T(8,128)(2,1)}), bf16[8,448,128]{2,1,0:T(8,128)(2,1)}, u32[]{:S(2)}, u32[]{:S(2)}) async-start(bf16[8,448,128]{2,1,0:T(8,128)(2,1)} %bitcast.16), calls=%async_computation.1 | async-start | bytes 1835008 | tf_op jit(solution)/shard_map/all_to_all | solution.py:90
  42.7 1.4 maximum_bitcast_fusion
  44.1 2.7 %copy.58 = bf16[256,3584]{1,0:T(8,128)(2,1)} copy(bf16[256,3584]{0,1:T(8,128)(2,1)S(1)} %maximum_bitcast_fusion) | data formatting | bytes 3670016 | tf_op jit(solution)/shard_map/dot_general | solution.py:62
  46.8 21.7 %all-gather.3.cloned.1.call-done = bf16[5,64,3584]{2,1,0:T(8,128)(2,1)} async-done(((bf16[5,8,3584]{2,1,0:T(8,128)(2,1)}), bf16[5,64,3584]{2,1,0:T(8,128)(2,1)}) %all-gather.3.cloned.1.call-update) | async-done | bytes 2293776 | tf_op jit(solution)/shard_map/all_gather | solution.py:57
  68.5 3.0 %fusion.33 = (bf16[2,320,128]{2,1,0:T(8,128)(2,1)S(1)}, f32[2,320,128]{2,1,0:T(8,128)S(1)}) fusion(bf16[320,3584,1]{1,0,2:T(8,128)(2,1)} %bitcast.110, bf16[2,128,3584]{2,1,0:T(8,128)(2,1)} %bitcast.100), kind=kOutput, calls=%fused_computation.77 | convolution fusion | flops 587284480 | bytes 4620288 | tf_op jit(solution)/shard_map/dot_general | solution.py:62
  71.5 2.3 collective-permute-start
  73.8 5.1 %collective-permute-done = bf16[2,320,128]{2,1,0:T(8,128)(2,1)S(1)} collective-permute-done((bf16[2,320,128]{2,1,0:T(8,128)(2,1)S(1)}, bf16[2,320,128]{2,1,0:T(8,128)(2,1)S(1)}, u32[]{:S(2)}, u32[]{:S(2)}) %collective-permute-start) | collective-permute-done | bytes 163872 | tf_op jit(solution)/shard_map/ppermute | solution.py:14
  79.0 17.6 %all_gather.13 = bf16[320,1024]{1,0:T(8,128)(2,1)S(1)} all-gather(bf16[320,128]{1,0:T(8,128)(2,1)S(1)} %fusion.19), channel_id=1, replica_groups=mesh['section'=8,'eg'=4,'q'=8,'dp'=2] {'q'}, dimensions={1}, use_global_device_ids=true | all-gather | bytes 737280 | tf_op jit(solution)/shard_map/all_gather | solution.py:66
  96.6 1.7 convolution_convert_fusion.3
  98.7 1.4 reshape.131
  100.1 6.1 %all-to-all-start.2 = ((bf16[64,2,1120]{2,1,0:T(2,128)(2,1)}), bf16[64,2,1120]{2,1,0:T(2,128)(2,1)S(1)}, u32[]{:S(2)}, u32[]{:S(2)}) async-start(bf16[64,2,1120]{2,1,0:T(2,128)(2,1)} %reshape.131), calls=%async_computation.2 | async-start | bytes 589824 | tf_op jit(solution)/shard_map/all_to_all | solution.py:72
  106.4 13.8 %all-to-all-done.2 = bf16[64,2,1120]{2,1,0:T(2,128)(2,1)S(1)} async-done(((bf16[64,2,1120]{2,1,0:T(2,128)(2,1)}), bf16[64,2,1120]{2,1,0:T(2,128)(2,1)S(1)}, u32[]{:S(2)}, u32[]{:S(2)}) %all-to-all-start.2) | async-done | bytes 286752 | tf_op jit(solution)/shard_map/all_to_all | solution.py:72
  123.1 3.1 %collective-permute-start.1 = (bf16[8,7168]{1,0:T(8,128)(2,1)S(1)}, bf16[8,7168]{1,0:T(8,128)(2,1)S(1)}, u32[]{:S(2)}, u32[]{:S(2)}) collective-permute-start(bf16[8,7168]{1,0:T(8,128)(2,1)S(1)} %fusion.15), channel_id=1, source_target_pairs={{0,64},{64,128},{128,192},{192,256},{256,320},{320,384},{384,448},... | collective-permute-start | bytes 344072 | tf_op jit(solution)/shard_map/ppermute | solution.py:14
  126.3 4.7 %collective-permute-done.1 = bf16[8,7168]{1,0:T(8,128)(2,1)S(1)} collective-permute-done((bf16[8,7168]{1,0:T(8,128)(2,1)S(1)}, bf16[8,7168]{1,0:T(8,128)(2,1)S(1)}, u32[]{:S(2)}, u32[]{:S(2)}) %collective-permute-start.1) | collective-permute-done | bytes 114720 | tf_op jit(solution)/shard_map/ppermute | solution.py:14
  131.9 12.6 %all_to_all.26 = bf16[8,2,8960]{2,1,0:T(2,128)(2,1)S(1)} all-to-all(bf16[8,2,8960]{2,1,0:T(2,128)(2,1)S(1)} %reshape.134), channel_id=1, replica_groups=mesh['section'=8,'eg'=4,'q'=8,'dp'=2] {'eg','dp'}, dimensions={0} | all-to-all | bytes 573440 | tf_op jit(solution)/shard_map/all_to_all | solution.py:55
  145.5 30.4 %all-gather.5.cloned.1.call-done = bf16[5,64,3584]{2,1,0:T(8,128)(2,1)} async-done(((bf16[5,8,3584]{2,1,0:T(8,128)(2,1)}), bf16[5,64,3584]{2,1,0:T(8,128)(2,1)}) %all-gather.5.cloned.1.call-update) | async-done | bytes 2293776 | tf_op jit(solution)/shard_map/all_gather | solution.py:57
  175.9 2.4 %fusion.34 = (bf16[2,320,128]{2,1,0:T(8,128)(2,1)S(1)}, f32[2,320,128]{2,1,0:T(8,128)S(1)}) fusion(bf16[320,3584,1]{1,0,2:T(8,128)(2,1)} %bitcast.111, bf16[2,128,3584]{2,1,0:T(8,128)(2,1)S(1)} %bitcast.101), kind=kOutput, calls=%fused_computation.78 | convolution fusion | flops 587284480 | bytes 4620288 | tf_op jit(solution)/shard_map/dot_general | solution.py:62
  178.3 2.2 collective-permute-start.2
  180.5 5.2 %collective-permute-done.2 = bf16[2,320,128]{2,1,0:T(8,128)(2,1)S(1)} collective-permute-done((bf16[2,320,128]{2,1,0:T(8,128)(2,1)S(1)}, bf16[2,320,128]{2,1,0:T(8,128)(2,1)S(1)}, u32[]{:S(2)}, u32[]{:S(2)}) %collective-permute-start.2) | collective-permute-done | bytes 163872 | tf_op jit(solution)/shard_map/ppermute | solution.py:14
  185.8 17.7 %all_gather.15 = bf16[320,1024]{1,0:T(8,128)(2,1)S(1)} all-gather(bf16[320,128]{1,0:T(8,128)(2,1)S(1)} %fusion.17), channel_id=1, replica_groups=mesh['section'=8,'eg'=4,'q'=8,'dp'=2] {'q'}, dimensions={1}, use_global_device_ids=true | all-gather | bytes 737280 | tf_op jit(solution)/shard_map/all_gather | solution.py:66
  203.5 1.7 convolution_convert_fusion.2
  207.0 7.8 %all-to-all-start.4 = ((bf16[64,2,1120]{2,1,0:T(2,128)(2,1)}), bf16[64,2,1120]{2,1,0:T(2,128)(2,1)S(1)}, u32[]{:S(2)}, u32[]{:S(2)}) async-start(bf16[64,2,1120]{2,1,0:T(2,128)(2,1)} %reshape.138), calls=%async_computation.4 | async-start | bytes 589824 | tf_op jit(solution)/shard_map/all_to_all | solution.py:72
  214.8 13.8 %all-to-all-done.4 = bf16[64,2,1120]{2,1,0:T(2,128)(2,1)S(1)} async-done(((bf16[64,2,1120]{2,1,0:T(2,128)(2,1)}), bf16[64,2,1120]{2,1,0:T(2,128)(2,1)S(1)}, u32[]{:S(2)}, u32[]{:S(2)}) %all-to-all-start.4) | async-done | bytes 286752 | tf_op jit(solution)/shard_map/all_to_all | solution.py:72
  (79 shorter events, 17.1 us)
Async XLA Ops:
  6.5 62.0 %all-gather.3.cloned.1.call-start = ((), (), s32[]{:S(2)}) async-start(), calls=%async_computation.5 | async-start | bytes 2580480 | tf_op jit(solution)/shard_map/all_gather | solution.py:57
  11.6 31.2 %copy-start.2 = (bf16[1,3584,128]{2,1,0:T(8,128)(2,1)S(1)}, bf16[1,3584,128]{2,1,0:T(8,128)(2,1)}, u32[]{:S(2)}) copy-start(bf16[1,3584,128]{2,1,0:T(8,128)(2,1)} %param.12) | copy-start | bytes 2752516
  34.6 62.0 %all-to-all-start.1 = ((bf16[8,448,128]{2,1,0:T(8,128)(2,1)}), bf16[8,448,128]{2,1,0:T(8,128)(2,1)}, u32[]{:S(2)}, u32[]{:S(2)}) async-start(bf16[8,448,128]{2,1,0:T(8,128)(2,1)} %bitcast.16), calls=%async_computation.1 | async-start | bytes 1835008 | tf_op jit(solution)/shard_map/all_to_all | solution.py:90
  71.5 7.4 %collective-permute-start = (bf16[2,320,128]{2,1,0:T(8,128)(2,1)S(1)}, bf16[2,320,128]{2,1,0:T(8,128)(2,1)S(1)}, u32[]{:S(2)}, u32[]{:S(2)}) collective-permute-start(bf16[2,320,128]{2,1,0:T(8,128)(2,1)S(1)} %get-tuple-element.16), channel_id=1, source_target_pairs={{0,1},{1,0},{2,3},{3,2},{4,5},{5,4},{6,7},{7,6},{8,9},{9,8},{10,11... | collective-permute-start | bytes 491528 | tf_op jit(solution)/shard_map/ppermute | solution.py:14
  96.6 9.6 %copy-start.4 = (f32[1,2,8,2]{2,3,1,0:T(2,128)S(1)}, f32[1,2,8,2]{2,3,1,0:T(2,128)}, u32[]{:S(2)}) copy-start(f32[1,2,8,2]{2,3,1,0:T(2,128)} %param.15) | copy-start | bytes 388
  100.1 20.1 %all-to-all-start.2 = ((bf16[64,2,1120]{2,1,0:T(2,128)(2,1)}), bf16[64,2,1120]{2,1,0:T(2,128)(2,1)S(1)}, u32[]{:S(2)}, u32[]{:S(2)}) async-start(bf16[64,2,1120]{2,1,0:T(2,128)(2,1)} %reshape.131), calls=%async_computation.2 | async-start | bytes 589824 | tf_op jit(solution)/shard_map/all_to_all | solution.py:72
  106.2 69.7 %all-gather.5.cloned.1.call-start = ((), (), s32[]{:S(2)}) async-start(), calls=%async_computation.6 | async-start | bytes 2580480 | tf_op jit(solution)/shard_map/all_gather | solution.py:57
  121.3 1.7 copy-start.1
  121.3 9.8 %copy-start.3 = (f32[1,7168]{1,0:T(1,128)S(1)}, f32[1,7168]{1,0:T(1,128)}, u32[]{:S(2)}) copy-start(f32[1,7168]{1,0:T(1,128)} %param.10) | copy-start | bytes 86020
  123.1 7.9 %collective-permute-start.1 = (bf16[8,7168]{1,0:T(8,128)(2,1)S(1)}, bf16[8,7168]{1,0:T(8,128)(2,1)S(1)}, u32[]{:S(2)}, u32[]{:S(2)}) collective-permute-start(bf16[8,7168]{1,0:T(8,128)(2,1)S(1)} %fusion.15), channel_id=1, source_target_pairs={{0,64},{64,128},{128,192},{192,256},{256,320},{320,384},{384,448},... | collective-permute-start | bytes 344072 | tf_op jit(solution)/shard_map/ppermute | solution.py:14
  131.2 44.7 %copy-start = (bf16[256,3584]{1,0:T(8,128)(2,1)S(1)}, bf16[256,3584]{1,0:T(8,128)(2,1)}, u32[]{:S(2)}) copy-start(bf16[256,3584]{1,0:T(8,128)(2,1)} %copy.58) | copy-start | bytes 5505028
  178.3 7.4 %collective-permute-start.2 = (bf16[2,320,128]{2,1,0:T(8,128)(2,1)S(1)}, bf16[2,320,128]{2,1,0:T(8,128)(2,1)S(1)}, u32[]{:S(2)}, u32[]{:S(2)}) collective-permute-start(bf16[2,320,128]{2,1,0:T(8,128)(2,1)S(1)} %get-tuple-element.18), channel_id=1, source_target_pairs={{0,1},{1,0},{2,3},{3,2},{4,5},{5,4},{6,7},{7,6},{8,9},{9,8},{10,11... | collective-permute-start | bytes 491528 | tf_op jit(solution)/shard_map/ppermute | solution.py:14
  207.0 21.7 %all-to-all-start.4 = ((bf16[64,2,1120]{2,1,0:T(2,128)(2,1)}), bf16[64,2,1120]{2,1,0:T(2,128)(2,1)S(1)}, u32[]{:S(2)}, u32[]{:S(2)}) async-start(bf16[64,2,1120]{2,1,0:T(2,128)(2,1)} %reshape.138), calls=%async_computation.4 | async-start | bytes 589824 | tf_op jit(solution)/shard_map/all_to_all | solution.py:72
Sparse Core Ops, SparseCore 0:
  34.8 33.7 all-gather.2
  145.6 30.2 all-gather.4
where the time goes:
time: 240 us; the launch traced here: 239 us
  waiting for transfers between devices  94.7 us (39%)
  blocking collectives  69.8 us (29%)
  starting transfers between devices  29.6 us (12%)
  local copies, waits for them, and re-layouts  14.7 us (6%)
  between operations  13.8 us (6%)
  matrix products  10.6 us (4%)
  other arithmetic  5.94 us (2%)
    all_gather x2, waiting for transfers between devices, moe_layer(): arrived = lax.all_gather(arrived, 'q', axis=1, tiled=True)  52.1 us
    all_gather x2, blocking collectives, moe_layer(): hidden_all = lax.all_gather(hidden, 'q', axis=1, tiled=True)  35.3 us
    all_to_all x2, blocking collectives, moe_layer(): lax.all_to_all(send, ('eg', 'dp'), split_axis=0, concat_axis=0, tiled=True)  34.5 us
    all_to_all x2, waiting for transfers between devices, moe_layer(): lax.all_to_all(out.reshape(sources, 2, capacity * piece // 2), ALL, split...  27.6 us
    ppermute x3, waiting for transfers between devices, passed_along(): lax.ppermute(array, axis, [(i, (i + by) % length) for i in range(length)])  14.9 us
    all_to_all x2, starting transfers between devices, moe_layer(): lax.all_to_all(out.reshape(sources, 2, capacity * piece // 2), ALL, split...  13.9 us
    all_to_all x1, starting transfers between devices, on_device(): lax.all_to_all(down_local.reshape(n_blocks, piece, width), 'q', split_axi...  8.1 us
    ppermute x3, starting transfers between devices, passed_along(): lax.ppermute(array, axis, [(i, (i + by) % length) for i in range(length)])  7.56 us
  transfers between devices with their start and end apart: 8, of which 7 were waited for; matrix products, arithmetic and copies ran while one was open for 3% of the time, Pallas kernels for 0%

commit v1 on v0

--- a/solution.py
+++ b/solution.py
@@ -63,7 +63,14 @@
     mine = gate_up.reshape(rows.shape[0], 2, units).transpose(1, 0, 2)
     both = mine + passed_along(mine.astype(jnp.bfloat16), "dp", 1).astype(jnp.float32)
     hidden = (jax.nn.silu(both[0]) * both[1]).astype(jnp.bfloat16)
-    hidden_all = lax.all_gather(hidden, "q", axis=1, tiled=True)
+
+    def divide_state(field_in):
+        everything = jnp.stack(lax.psum(1, axis_name="q") * [field_in])
+        return jnp.concatenate(
+            lax.all_to_all(everything, axis_name="q", concat_axis=0, split_axis=0), 1
+        )
+
+    hidden_all = divide_state(hidden)
     out = lax.dot_general(
         hidden_all, down_mine, (((1,), (1,)), ((), ())), preferred_element_type=jnp.float32
     ).astype(jnp.bfloat16)

time: 240 us -> 239 us (level)
  blocking collectives: 69.8 us -> 67 us
    all_gather x2 -> x0, blocking collectives: 35.3 us -> none  [moe_layer(): hidden_all = lax.all_gather(hidden, 'q', axis=1, tiled=True)]
    all_to_all x0 -> x2, blocking collectives: none -> 32.5 us  [divide_state(): lax.all_to_all(everything, axis_name='q', concat_axis=0, split_axis=0)]
where the time goes in v1:
time: 239 us; the launch traced here: 238 us
  waiting for transfers between devices  94.7 us (40%)
  blocking collectives  67 us (28%)
  starting transfers between devices  31.4 us (13%)
  local copies, waits for them, and re-layouts  14.9 us (6%)
  between operations  13.8 us (6%)
  matrix products  10.7 us (4%)
  other arithmetic  5.94 us (2%)
    all_gather x2, waiting for transfers between devices, moe_layer(): arrived = lax.all_gather(arrived, 'q', axis=1, tiled=True)  52.1 us
    all_to_all x2, blocking collectives, moe_layer(): lax.all_to_all(send, ('eg', 'dp'), split_axis=0, concat_axis=0, tiled=True)  34.5 us
    all_to_all x2, blocking collectives, divide_state(): lax.all_to_all(everything, axis_name='q', concat_axis=0, split_axis=0)  32.5 us
    all_to_all x2, waiting for transfers between devices, moe_layer(): lax.all_to_all(out.reshape(sources, 2, capacity * piece // 2), ALL, split...  27.6 us
    all_to_all x2, starting transfers between devices, moe_layer(): lax.all_to_all(out.reshape(sources, 2, capacity * piece // 2), ALL, split...  15.7 us
    ppermute x3, waiting for transfers between devices, passed_along(): lax.ppermute(array, axis, [(i, (i + by) % length) for i in range(length)])  14.9 us
    all_to_all x1, starting transfers between devices, on_device(): lax.all_to_all(down_local.reshape(n_blocks, piece, width), 'q', split_axi...  8.1 us
    ppermute x3, starting transfers between devices, passed_along(): lax.ppermute(array, axis, [(i, (i + by) % length) for i in range(length)])  7.57 us
  transfers between devices with their start and end apart: 8, of which 7 were waited for; matrix products, arithmetic and copies ran while one was open for 3% of the time, Pallas kernels for 0%

profile of v1, /device:TPU:1, one launch (start us, length us, event | category | flops | bytes accessed | tf_op | source)
XLA Modules:
  0.0 238.3 jit_solution(16449250978074075804)
XLA Ops:
  11.7 21.9 %all_to_all.35 = bf16[8,2,8960]{2,1,0:T(2,128)(2,1)S(1)} all-to-all(bf16[8,2,8960]{2,1,0:T(2,128)(2,1)S(1)} %reshape.134), channel_id=1, replica_groups=mesh['section'=8,'eg'=4,'q'=8,'dp'=2] {'eg','dp'}, dimensions={0} | all-to-all | bytes 573440 | tf_op jit(solution)/shard_map/all_to_all | solution.py:55
  34.6 8.1 %all-to-all-start.2 = ((bf16[8,448,128]{2,1,0:T(8,128)(2,1)}), bf16[8,448,128]{2,1,0:T(8,128)(2,1)}, u32[]{:S(2)}, u32[]{:S(2)}) async-start(bf16[8,448,128]{2,1,0:T(8,128)(2,1)} %bitcast.16), calls=%async_computation.2 | async-start | bytes 1835008 | tf_op jit(solution)/shard_map/all_to_all | solution.py:97
  42.7 1.4 maximum_bitcast_fusion
  44.1 2.7 %copy.56 = bf16[256,3584]{1,0:T(8,128)(2,1)} copy(bf16[256,3584]{0,1:T(8,128)(2,1)S(1)} %maximum_bitcast_fusion) | data formatting | bytes 3670016 | tf_op jit(solution)/shard_map/dot_general | solution.py:62
  46.8 21.7 %all-gather.3.cloned.1.call-done = bf16[5,64,3584]{2,1,0:T(8,128)(2,1)} async-done(((bf16[5,8,3584]{2,1,0:T(8,128)(2,1)}), bf16[5,64,3584]{2,1,0:T(8,128)(2,1)}) %all-gather.3.cloned.1.call-update) | async-done | bytes 2293776 | tf_op jit(solution)/shard_map/all_gather | solution.py:57
  68.5 3.0 %fusion.35 = (bf16[2,320,128]{2,1,0:T(8,128)(2,1)S(1)}, f32[2,320,128]{2,1,0:T(8,128)S(1)}) fusion(bf16[320,3584,1]{1,0,2:T(8,128)(2,1)} %bitcast.98, bf16[2,128,3584]{2,1,0:T(8,128)(2,1)} %bitcast.88), kind=kOutput, calls=%fused_computation.77 | convolution fusion | flops 587284480 | bytes 4620288 | tf_op jit(solution)/shard_map/dot_general | solution.py:62
  71.5 2.3 collective-permute-start
  73.8 5.1 %collective-permute-done = bf16[2,320,128]{2,1,0:T(8,128)(2,1)S(1)} collective-permute-done((bf16[2,320,128]{2,1,0:T(8,128)(2,1)S(1)}, bf16[2,320,128]{2,1,0:T(8,128)(2,1)S(1)}, u32[]{:S(2)}, u32[]{:S(2)}) %collective-permute-start) | collective-permute-done | bytes 163872 | tf_op jit(solution)/shard_map/ppermute | solution.py:14
  79.1 16.6 %all_to_all.36 = bf16[8,320,128]{2,1,0:T(8,128)(2,1)S(1)} all-to-all(bf16[8,320,128]{2,1,0:T(8,128)(2,1)S(1)} %stack.9), channel_id=1, replica_groups=mesh['section'=8,'eg'=4,'q'=8,'dp'=2] {'q'}, dimensions={0} | all-to-all | bytes 1310720 | tf_op jit(solution)/shard_map/all_to_all | solution.py:70
  95.7 1.7 fusion
  97.7 1.4 reshape.139
  99.1 6.6 %all-to-all-start.3 = ((bf16[64,2,1120]{2,1,0:T(2,128)(2,1)}), bf16[64,2,1120]{2,1,0:T(2,128)(2,1)S(1)}, u32[]{:S(2)}, u32[]{:S(2)}) async-start(bf16[64,2,1120]{2,1,0:T(2,128)(2,1)} %reshape.139), calls=%async_computation.3 | async-start | bytes 589824 | tf_op jit(solution)/shard_map/all_to_all | solution.py:79
  105.9 13.8 %all-to-all-done.3 = bf16[64,2,1120]{2,1,0:T(2,128)(2,1)S(1)} async-done(((bf16[64,2,1120]{2,1,0:T(2,128)(2,1)}), bf16[64,2,1120]{2,1,0:T(2,128)(2,1)S(1)}, u32[]{:S(2)}, u32[]{:S(2)}) %all-to-all-start.3) | async-done | bytes 286752 | tf_op jit(solution)/shard_map/all_to_all | solution.py:79
  122.7 3.1 %collective-permute-start.1 = (bf16[8,7168]{1,0:T(8,128)(2,1)S(1)}, bf16[8,7168]{1,0:T(8,128)(2,1)S(1)}, u32[]{:S(2)}, u32[]{:S(2)}) collective-permute-start(bf16[8,7168]{1,0:T(8,128)(2,1)S(1)} %fusion.17), channel_id=1, source_target_pairs={{0,64},{64,128},{128,192},{192,256},{256,320},{320,384},{384,448},... | collective-permute-start | bytes 344072 | tf_op jit(solution)/shard_map/ppermute | solution.py:14
  125.9 4.7 %collective-permute-done.1 = bf16[8,7168]{1,0:T(8,128)(2,1)S(1)} collective-permute-done((bf16[8,7168]{1,0:T(8,128)(2,1)S(1)}, bf16[8,7168]{1,0:T(8,128)(2,1)S(1)}, u32[]{:S(2)}, u32[]{:S(2)}) %collective-permute-start.1) | collective-permute-done | bytes 114720 | tf_op jit(solution)/shard_map/ppermute | solution.py:14
  131.5 12.6 %all_to_all.37 = bf16[8,2,8960]{2,1,0:T(2,128)(2,1)S(1)} all-to-all(bf16[8,2,8960]{2,1,0:T(2,128)(2,1)S(1)} %reshape.142), channel_id=1, replica_groups=mesh['section'=8,'eg'=4,'q'=8,'dp'=2] {'eg','dp'}, dimensions={0} | all-to-all | bytes 573440 | tf_op jit(solution)/shard_map/all_to_all | solution.py:55
  145.1 30.4 %all-gather.5.cloned.1.call-done = bf16[5,64,3584]{2,1,0:T(8,128)(2,1)} async-done(((bf16[5,8,3584]{2,1,0:T(8,128)(2,1)}), bf16[5,64,3584]{2,1,0:T(8,128)(2,1)}) %all-gather.5.cloned.1.call-update) | async-done | bytes 2293776 | tf_op jit(solution)/shard_map/all_gather | solution.py:57
  175.5 2.4 %fusion.36 = (bf16[2,320,128]{2,1,0:T(8,128)(2,1)S(1)}, f32[2,320,128]{2,1,0:T(8,128)S(1)}) fusion(bf16[320,3584,1]{1,0,2:T(8,128)(2,1)} %bitcast.99, bf16[2,128,3584]{2,1,0:T(8,128)(2,1)S(1)} %bitcast.89), kind=kOutput, calls=%fused_computation.78 | convolution fusion | flops 587284480 | bytes 4620288 | tf_op jit(solution)/shard_map/dot_general | solution.py:62
  177.9 2.2 collective-permute-start.2
  180.1 5.1 %collective-permute-done.2 = bf16[2,320,128]{2,1,0:T(8,128)(2,1)S(1)} collective-permute-done((bf16[2,320,128]{2,1,0:T(8,128)(2,1)S(1)}, bf16[2,320,128]{2,1,0:T(8,128)(2,1)S(1)}, u32[]{:S(2)}, u32[]{:S(2)}) %collective-permute-start.2) | collective-permute-done | bytes 163872 | tf_op jit(solution)/shard_map/ppermute | solution.py:14
  185.5 15.9 %all_to_all.38 = bf16[8,320,128]{2,1,0:T(8,128)(2,1)S(1)} all-to-all(bf16[8,320,128]{2,1,0:T(8,128)(2,1)S(1)} %stack.11), channel_id=1, replica_groups=mesh['section'=8,'eg'=4,'q'=8,'dp'=2] {'q'}, dimensions={0} | all-to-all | bytes 1310720 | tf_op jit(solution)/shard_map/all_to_all | solution.py:70
  201.4 1.7 fusion.1
  204.8 9.1 %all-to-all-start.6 = ((bf16[64,2,1120]{2,1,0:T(2,128)(2,1)}), bf16[64,2,1120]{2,1,0:T(2,128)(2,1)S(1)}, u32[]{:S(2)}, u32[]{:S(2)}) async-start(bf16[64,2,1120]{2,1,0:T(2,128)(2,1)} %reshape.147), calls=%async_computation.6 | async-start | bytes 589824 | tf_op jit(solution)/shard_map/all_to_all | solution.py:79
  214.0 13.8 %all-to-all-done.6 = bf16[64,2,1120]{2,1,0:T(2,128)(2,1)S(1)} async-done(((bf16[64,2,1120]{2,1,0:T(2,128)(2,1)}), bf16[64,2,1120]{2,1,0:T(2,128)(2,1)S(1)}, u32[]{:S(2)}, u32[]{:S(2)}) %all-to-all-start.6) | async-done | bytes 286752 | tf_op jit(solution)/shard_map/all_to_all | solution.py:79
  (81 shorter events, 17.3 us)
Async XLA Ops:
  6.5 62.0 %all-gather.3.cloned.1.call-start = ((), (), s32[]{:S(2)}) async-start(), calls=%async_computation.7 | async-start | bytes 2580480 | tf_op jit(solution)/shard_map/all_gather | solution.py:57
  11.6 31.2 %copy-start.2 = (bf16[1,3584,128]{2,1,0:T(8,128)(2,1)S(1)}, bf16[1,3584,128]{2,1,0:T(8,128)(2,1)}, u32[]{:S(2)}) copy-start(bf16[1,3584,128]{2,1,0:T(8,128)(2,1)} %param.12) | copy-start | bytes 2752516
  34.6 44.4 %all-to-all-start.2 = ((bf16[8,448,128]{2,1,0:T(8,128)(2,1)}), bf16[8,448,128]{2,1,0:T(8,128)(2,1)}, u32[]{:S(2)}, u32[]{:S(2)}) async-start(bf16[8,448,128]{2,1,0:T(8,128)(2,1)} %bitcast.16), calls=%async_computation.2 | async-start | bytes 1835008 | tf_op jit(solution)/shard_map/all_to_all | solution.py:97
  71.5 7.4 %collective-permute-start = (bf16[2,320,128]{2,1,0:T(8,128)(2,1)S(1)}, bf16[2,320,128]{2,1,0:T(8,128)(2,1)S(1)}, u32[]{:S(2)}, u32[]{:S(2)}) collective-permute-start(bf16[2,320,128]{2,1,0:T(8,128)(2,1)S(1)} %get-tuple-element.16), channel_id=1, source_target_pairs={{0,1},{1,0},{2,3},{3,2},{4,5},{5,4},{6,7},{7,6},{8,9},{9,8},{10,11... | collective-permute-start | bytes 491528 | tf_op jit(solution)/shard_map/ppermute | solution.py:14
  95.7 10.2 %copy-start.4 = (f32[1,2,8,2]{2,3,1,0:T(2,128)S(1)}, f32[1,2,8,2]{2,3,1,0:T(2,128)}, u32[]{:S(2)}) copy-start(f32[1,2,8,2]{2,3,1,0:T(2,128)} %param.15) | copy-start | bytes 388
  99.1 20.6 %all-to-all-start.3 = ((bf16[64,2,1120]{2,1,0:T(2,128)(2,1)}), bf16[64,2,1120]{2,1,0:T(2,128)(2,1)S(1)}, u32[]{:S(2)}, u32[]{:S(2)}) async-start(bf16[64,2,1120]{2,1,0:T(2,128)(2,1)} %reshape.139), calls=%async_computation.3 | async-start | bytes 589824 | tf_op jit(solution)/shard_map/all_to_all | solution.py:79
  105.8 69.7 %all-gather.5.cloned.1.call-start = ((), (), s32[]{:S(2)}) async-start(), calls=%async_computation.8 | async-start | bytes 2580480 | tf_op jit(solution)/shard_map/all_gather | solution.py:57
  120.9 1.7 copy-start.1
  120.9 9.8 %copy-start.3 = (f32[1,7168]{1,0:T(1,128)S(1)}, f32[1,7168]{1,0:T(1,128)}, u32[]{:S(2)}) copy-start(f32[1,7168]{1,0:T(1,128)} %param.10) | copy-start | bytes 86020
  122.7 7.9 %collective-permute-start.1 = (bf16[8,7168]{1,0:T(8,128)(2,1)S(1)}, bf16[8,7168]{1,0:T(8,128)(2,1)S(1)}, u32[]{:S(2)}, u32[]{:S(2)}) collective-permute-start(bf16[8,7168]{1,0:T(8,128)(2,1)S(1)} %fusion.17), channel_id=1, source_target_pairs={{0,64},{64,128},{128,192},{192,256},{256,320},{320,384},{384,448},... | collective-permute-start | bytes 344072 | tf_op jit(solution)/shard_map/ppermute | solution.py:14
  130.8 44.7 %copy-start = (bf16[256,3584]{1,0:T(8,128)(2,1)S(1)}, bf16[256,3584]{1,0:T(8,128)(2,1)}, u32[]{:S(2)}) copy-start(bf16[256,3584]{1,0:T(8,128)(2,1)} %copy.56) | copy-start | bytes 5505028
  177.9 7.4 %collective-permute-start.2 = (bf16[2,320,128]{2,1,0:T(8,128)(2,1)S(1)}, bf16[2,320,128]{2,1,0:T(8,128)(2,1)S(1)}, u32[]{:S(2)}, u32[]{:S(2)}) collective-permute-start(bf16[2,320,128]{2,1,0:T(8,128)(2,1)S(1)} %get-tuple-element.18), channel_id=1, source_target_pairs={{0,1},{1,0},{2,3},{3,2},{4,5},{5,4},{6,7},{7,6},{8,9},{9,8},{10,11... | collective-permute-start | bytes 491528 | tf_op jit(solution)/shard_map/ppermute | solution.py:14
  204.8 23.0 %all-to-all-start.6 = ((bf16[64,2,1120]{2,1,0:T(2,128)(2,1)}), bf16[64,2,1120]{2,1,0:T(2,128)(2,1)S(1)}, u32[]{:S(2)}, u32[]{:S(2)}) async-start(bf16[64,2,1120]{2,1,0:T(2,128)(2,1)} %reshape.147), calls=%async_computation.6 | async-start | bytes 589824 | tf_op jit(solution)/shard_map/all_to_all | solution.py:79
Sparse Core Ops, SparseCore 0:
  34.8 33.7 all-gather.2
  145.2 30.2 all-gather.4
